TPU v7x, 32 devices: a whole 2x2x4 slice. The times are simulated.
32 devices in a mesh: leaf: 4 (over y, x), src: 8 (over z, core).
Axes of the slice: x: 2, y: 2, z: 4, core: 2. Of those that a mesh axis runs over, the one named last changes fastest.
Arguments:
- src_cells: int32 [1024], P('src'), may hold values from 0 to 2047
- rec_cells: int32 [512], P('leaf'), may hold values from 0 to 511
- residual: float32 [1024, 512], P('src', 'leaf'), may hold values from -6 to 6
- pattern: int32 [12, 2], P('leaf'), may hold values 0 or 1
- leaf_lower: bfloat16 [2048, 512], P('leaf'), may hold values from -0.1875 to 0.1875
- leaf_upper: bfloat16 [2048, 512], P('leaf'), may hold values from -0.1875 to 0.1875
- leaf_inv: bfloat16 [16, 128, 128], P('leaf'), may hold values from -0.5 to 0.5
- anc_lower: bfloat16 [1024, 512], P('leaf'), may hold values from -0.125 to 0.125
- anc_upper: bfloat16 [2048, 256], P('leaf'), may hold values from -0.375 to 0.375
- sep_inv: bfloat16 [8, 128, 128], P('leaf'), may hold values from -0.5 to 0.5
- sep_lower: bfloat16 [8, 256, 128], P('leaf'), may hold values from -0.25 to 0.25
- sep_upper: bfloat16 [8, 128, 256], P('leaf'), may hold values from -0.375 to 0.375
Outputs:
- forward_field: float32 [1024, 2048], P('src', 'leaf')
- adjoint_field: float32 [1024, 2048], P('src', 'leaf')
- gradient: float32 [2048], P(('leaf', 'src'))
Inputs may be any that keep to these rules, and one draw needn't show every extreme that they name: src_cells holds 512 d + c for a source in interior cell c of subdomain d. rec_cells holds a receiver's cell within the subdomain of its block of 128 entries.
All inputs are finite; a program needn't handle non-finite values. No bound on the sum of `pattern` on one device may be relied on, other than what follows from the above.
Results may differ from a plain program's by a relative error of at most 0.0068.
Values may be sent and summed in bfloat16 or wider, within the bound.
No kernel may reach another device: no remote copies, remote signals or barrier semaphores. Data moves between devices by JAX's collectives and lax.ppermute only.
A program may use at most 64 MiB of HBM per device.

v0:
```python
import math
import jax
import jax.numpy as jnp
from jax import lax
from jax.sharding import PartitionSpec as P


def across(former, latter):
    return lax.dot_general(
        former, latter, (((1,), (1,)), ((), ())), preferred_element_type=jnp.float32
    )


def plain_dot(former, latter):
    return jnp.dot(former, latter, preferred_element_type=jnp.float32)


def as_half(values):
    return values.astype(jnp.bfloat16)


def lower_solve(right_side, lower, block_size, block_count):
    solved = []
    for index in range(block_count):
        segment = right_side[:, index * block_size : (index + 1) * block_size]
        if index:
            earlier = as_half(jnp.concatenate(solved, axis=1))
            segment = segment - across(
                earlier, lower[index * block_size : (index + 1) * block_size, : index * block_size]
            )
        solved.append(segment)
    return jnp.concatenate(solved, axis=1)


def upper_solve(right_side, upper, inverse, block_size, block_count):
    behind = []
    for index in reversed(range(block_count)):
        segment = right_side[:, index * block_size : (index + 1) * block_size]
        if behind:
            segment = segment - across(
                as_half(jnp.concatenate(behind, axis=1)),
                upper[index * block_size : (index + 1) * block_size, (index + 1) * block_size :],
            )
        behind.insert(0, across(as_half(segment), inverse[index]))
    return jnp.concatenate(behind, axis=1)


def upper_t_solve(right_side, upper, inverse, block_size, block_count):
    solved = []
    for index in range(block_count):
        segment = right_side[:, index * block_size : (index + 1) * block_size]
        if index:
            earlier = as_half(jnp.concatenate(solved, axis=1))
            segment = segment - plain_dot(
                earlier, upper[: index * block_size, index * block_size : (index + 1) * block_size]
            )
        solved.append(plain_dot(as_half(segment), inverse[index]))
    return jnp.concatenate(solved, axis=1)


def lower_t_solve(right_side, lower, block_size, block_count):
    behind = []
    for index in reversed(range(block_count)):
        segment = right_side[:, index * block_size : (index + 1) * block_size]
        if behind:
            segment = segment - plain_dot(
                as_half(jnp.concatenate(behind, axis=1)),
                lower[(index + 1) * block_size :, index * block_size : (index + 1) * block_size],
            )
        behind.insert(0, segment)
    return jnp.concatenate(behind, axis=1)


def climb(starts, handlers, levels, block_size, device):
    contributions = list(starts)
    results = [[] for member in starts]
    for height in range(1, levels + 1):
        lowest = (height - 1) * block_size
        piece = jnp.stack([summed[:, lowest : lowest + block_size] for summed in contributions])
        gathered = lax.all_gather(piece[None], "leaf", axis=0, tiled=True)
        first = device >> height << height
        total = jnp.sum(lax.dynamic_slice_in_dim(gathered, first, 1 << height, 0), axis=0)
        owner = device % (1 << height) == 0
        member = 0
        node_value, coupling = handlers[member](height, total[member])
        results[member].append(node_value)
        contributions[member] = contributions[member] + jnp.where(
            owner, coupling, jnp.zeros_like(coupling)
        )
    return results


def descend(node_values, handlers, levels, block_size, device, sources):
    known = [jnp.zeros((sources, levels * block_size), jnp.float32) for member in node_values]
    for height in range(levels, 0, -1):
        outgoing = jnp.stack([as_half(handlers[0](height, known[0], node_values[0][height - 1]))])
        gathered = lax.all_gather(outgoing[None], "leaf", axis=0, tiled=True)
        owner_index = device >> height << height
        piece = lax.dynamic_index_in_dim(gathered, owner_index, 0, keepdims=False).astype(
            jnp.float32
        )
        known = [lax.dynamic_update_slice_in_dim(known[0], piece[0], (height - 1) * block_size, 1)]
    return known


def shards(
    src_cells,
    rec_cells,
    residual,
    pattern,
    leaf_lower,
    leaf_upper,
    leaf_inv,
    anc_lower,
    anc_upper,
    sep_inv,
    sep_lower,
    sep_upper,
):
    levels = lax.axis_size("leaf").bit_length() - 1
    device = lax.axis_index("leaf")
    block_size = leaf_inv.shape[1]
    block_count = leaf_inv.shape[0]
    cell_count = leaf_lower.shape[1]
    source_count = src_cells.shape[0]
    factor = 1.0 / math.sqrt(source_count * lax.axis_size("src"))
    present = pattern.astype(jnp.float32)

    def level_mask(height):
        level_row = present[height] * (jnp.arange(1, levels + 1) > height).astype(jnp.float32)
        return jnp.repeat(level_row, block_size)

    columns = lax.broadcasted_iota(jnp.int32, (source_count, cell_count), 1)
    forcing = (src_cells[:, None] - device * cell_count == columns).astype(jnp.float32)
    receiver_hits = (
        rec_cells[:, None] == lax.broadcasted_iota(jnp.int32, (rec_cells.shape[0], cell_count), 1)
    ).astype(jnp.float32)
    adjoint_rhs = jnp.dot(residual, receiver_hits, precision=lax.Precision.HIGHEST)

    def forward_up(height, summed):
        node_value = -summed
        return (node_value, across(as_half(node_value), sep_lower[height - 1]) * level_mask(height))

    def adjoint_up(height, summed):
        node_value = plain_dot(as_half(-summed), sep_inv[height - 1])
        return (
            node_value,
            plain_dot(as_half(node_value), sep_upper[height - 1]) * level_mask(height),
        )

    def forward_down(height, above, node_value):
        right_side = node_value - across(as_half(above * level_mask(height)), sep_upper[height - 1])
        return across(as_half(right_side), sep_inv[height - 1])

    def adjoint_down(height, above, node_value):
        return node_value - plain_dot(as_half(above * level_mask(height)), sep_lower[height - 1])

    base_mask = level_mask(0)
    y_leaf = lower_solve(forcing, leaf_lower, block_size, block_count)
    forward_start = across(as_half(y_leaf), anc_lower) * base_mask
    z_leaf = upper_t_solve(adjoint_rhs, leaf_upper, leaf_inv, block_size, block_count)
    adjoint_start = plain_dot(as_half(z_leaf), anc_upper) * base_mask
    forward_values = climb([forward_start], [forward_up], levels, block_size, device)
    forward_above = descend(
        forward_values, [forward_down], levels, block_size, device, source_count
    )[0]
    adjoint_values = climb([adjoint_start], [adjoint_up], levels, block_size, device)
    adjoint_above = descend(
        adjoint_values, [adjoint_down], levels, block_size, device, source_count
    )[0]
    forward_remain = y_leaf - across(as_half(forward_above * base_mask), anc_upper)
    forward_field = upper_solve(forward_remain, leaf_upper, leaf_inv, block_size, block_count)
    adjoint_remain = z_leaf - plain_dot(as_half(adjoint_above * base_mask), anc_lower)
    adjoint_field = lower_t_solve(adjoint_remain, leaf_lower, block_size, block_count)
    partial_gradient = jnp.sum(forward_field * adjoint_field, axis=0)
    gradient = lax.psum_scatter(partial_gradient, "src", scatter_dimension=0, tiled=True) * factor
    return (forward_field, adjoint_field, gradient)


def solution(mesh):
    in_specs = (
        P("src"),
        P("leaf"),
        P("src", "leaf"),
        P("leaf", None),
        P("leaf", None),
        P("leaf", None),
        P("leaf", None, None),
        P("leaf", None),
        P("leaf", None),
        P("leaf", None, None),
        P("leaf", None, None),
        P("leaf", None, None),
    )
    out_specs = (P("src", "leaf"), P("src", "leaf"), P(("leaf", "src")))
    return jax.shard_map(shards, mesh=mesh, in_specs=in_specs, out_specs=out_specs, check_vma=False)
```

profile of v0, /device:TPU:0, one launch (start us, length us, event | category | flops | bytes accessed | tf_op | source)
XLA Modules:
  0.0 98.7 jit_solution(13294854775724279794)
XLA Ops:
  0.6 0.0 copy-start
  0.6 0.0 copy-start.7
  0.7 0.7 broadcast_subtract_fusion
  1.4 0.9 fusion.189
  2.3 0.0 copy-done.7
  2.4 0.1 fusion.190
  2.5 0.0 copy-start.5
  2.5 0.2 convolution_subtract_fusion.5
  2.7 0.0 copy-start.9
  2.7 0.7 copy-done.9
  3.4 0.2 slice_reduce_fusion
  3.6 0.1 broadcast_bitcast_fusion.1
  3.7 0.0 copy-done.5
  3.7 0.2 convolution_multiply_fusion.1
  3.9 0.0 copy-start.6
  4.0 10.6 %all-gather = f32[512,128]{1,0:T(8,128)S(1)} all-gather(f32[128,128]{1,0:T(8,128)S(1)} %slice.198), channel_id=2, replica_groups=mesh['leaf'=4,'src'=8] {'leaf'}, dimensions={0}, use_global_device_ids=true | all-gather | bytes 327680 | tf_op jit(solution)/shard_map/all_gather | solution.py:80
  14.5 0.0 copy-done.8
  14.6 0.0 copy-start.3
  14.6 0.4 convolution_bitcast_fusion
  15.0 0.5 copy-done.3
  15.5 0.2 fusion.180
  15.7 0.3 fusion.181
  16.0 0.4 fusion.184
  16.4 0.4 fusion.13
  16.8 0.0 copy-done
  16.8 0.2 convolution_multiply_fusion
  17.0 9.0 %all-gather.4 = f32[512,128]{1,0:T(8,128)S(1)} all-gather(f32[128,128]{1,0:T(8,128)S(1)} %slice.210), channel_id=6, replica_groups=mesh['leaf'=4,'src'=8] {'leaf'}, dimensions={0}, use_global_device_ids=true | all-gather | bytes 327680 | tf_op jit(solution)/shard_map/all_gather | solution.py:80
  26.0 0.0 copy-start.2
  26.0 0.8 copy-done.4
  26.8 0.1 fusion.121
  27.0 0.0 copy-done.2
  27.0 0.0 copy-start.1
  27.0 0.1 fusion.91
  27.1 0.8 copy-done.1
  27.9 0.2 fusion.98
  28.1 0.1 broadcast_bitcast_fusion
  28.2 8.1 %all-gather.1 = f32[512,128]{1,0:T(8,128)S(1)} all-gather(f32[128,128]{1,0:T(8,128)S(1)} %get-tuple-element.16), channel_id=3, replica_groups=mesh['leaf'=4,'src'=8] {'leaf'}, dimensions={0}, use_global_device_ids=true | all-gather | bytes 327680 | tf_op jit(solution)/shard_map/all_gather | solution.py:80
  36.3 0.1 broadcast_bitcast_fusion.2
  36.4 0.3 convolution_convert_fusion.1
  36.6 8.7 %all-gather.2 = bf16[512,128]{1,0:T(8,128)(2,1)S(1)} all-gather(bf16[128,128]{1,0:T(8,128)(2,1)S(1)} %convolution_convert_fusion.1), channel_id=4, replica_groups=mesh['leaf'=4,'src'=8] {'leaf'}, dimensions={0}, use_global_device_ids=true | all-gather | bytes 163840 | tf_op jit(solution)/shard_map/all_gather | solution.py:97
  45.4 0.3 convolution_convert_fusion
  45.7 7.3 %all-gather.3 = bf16[512,128]{1,0:T(8,128)(2,1)S(1)} all-gather(bf16[128,128]{1,0:T(8,128)(2,1)S(1)} %convolution_convert_fusion), channel_id=5, replica_groups=mesh['leaf'=4,'src'=8] {'leaf'}, dimensions={0}, use_global_device_ids=true | all-gather | bytes 163840 | tf_op jit(solution)/shard_map/all_gather | solution.py:97
  53.0 0.2 convolution_subtract_fusion.1
  53.2 0.1 fusion.193
  53.3 0.3 fusion.194
  53.6 0.3 fusion.197
  53.9 0.3 fusion.10
  54.2 9.2 %all-gather.5 = f32[512,128]{1,0:T(8,128)S(1)} all-gather(f32[128,128]{1,0:T(8,128)S(1)} %get-tuple-element.15), channel_id=7, replica_groups=mesh['leaf'=4,'src'=8] {'leaf'}, dimensions={0}, use_global_device_ids=true | all-gather | bytes 327680 | tf_op jit(solution)/shard_map/all_gather | solution.py:80
  63.5 0.1 fusion.122
  63.6 0.2 fusion.5
  63.7 7.3 %all-gather.6 = bf16[512,128]{1,0:T(8,128)(2,1)S(1)} all-gather(bf16[128,128]{1,0:T(8,128)(2,1)S(1)} %fusion.5), channel_id=8, replica_groups=mesh['leaf'=4,'src'=8] {'leaf'}, dimensions={0}, use_global_device_ids=true | all-gather | bytes 163840 | tf_op jit(solution)/shard_map/all_gather | solution.py:97
  71.1 0.1 fusion.6
  71.2 8.6 %all-gather.7 = bf16[512,128]{1,0:T(8,128)(2,1)S(1)} all-gather(bf16[128,128]{1,0:T(8,128)(2,1)S(1)} %fusion.6), channel_id=9, replica_groups=mesh['leaf'=4,'src'=8] {'leaf'}, dimensions={0}, use_global_device_ids=true | all-gather | bytes 163840 | tf_op jit(solution)/shard_map/all_gather | solution.py:97
  79.9 0.3 convolution_subtract_fusion
  80.1 0.2 fusion.191
  80.4 0.2 fusion.192
  80.6 0.2 convolution_subtract_fusion.8
  80.8 0.1 multiply_reduce_fusion
  81.0 0.8 copy.21
  81.8 0.8 copy.22
  82.7 13.6 %all-reduce.2 = f32[512]{0:T(512)S(1)} all-reduce(f32[512]{0:T(512)S(1)} %get-tuple-element.12), channel_id=10, replica_groups=mesh['leaf'=4,'src'=8] {'src'}, use_global_device_ids=true, to_apply=%region_5.6.clone | all-reduce | flops 512 | bytes 4096
  96.3 0.7 copy-done.11
  96.9 0.6 dynamic-slice
  98.1 0.6 dynamic-slice_multiply_fusion
  (26 shorter events, 0.2 us)
Async XLA Ops:
  0.6 16.1 %copy-start = (bf16[512,256]{1,0:T(8,128)(2,1)S(1)}, bf16[512,256]{1,0:T(8,128)(2,1)}, u32[]{:S(2)}) copy-start(bf16[512,256]{1,0:T(8,128)(2,1)} %param.20) | copy-start | bytes 786436
  0.6 1.7 %copy-start.7 = (bf16[512,512]{1,0:T(8,128)(2,1)S(1)}, bf16[512,512]{1,0:T(8,128)(2,1)}, u32[]{:S(2)}) copy-start(bf16[512,512]{1,0:T(8,128)(2,1)} %param.16) | copy-start | bytes 1572868
  2.5 1.2 %copy-start.5 = (bf16[256,512]{1,0:T(8,128)(2,1)S(1)}, bf16[256,512]{1,0:T(8,128)(2,1)}, u32[]{:S(2)}) copy-start(bf16[256,512]{1,0:T(8,128)(2,1)} %param.19) | copy-start | bytes 786436
  2.7 0.7 copy-start.9
  3.7 10.9 %copy-start.8 = (f32[128,128]{1,0:T(8,128)S(1)}, f32[128,128]{1,0:T(8,128)}, u32[]{:S(2)}) copy-start(f32[128,128]{1,0:T(8,128)} %param.14) | copy-start | bytes 196612
  3.7 10.9 %copy-start.10 = (s32[128]{0:T(128)S(1)}, s32[128]{0:T(128)}, u32[]{:S(2)}) copy-start(s32[128]{0:T(128)} %param.13) | copy-start | bytes 1540
  3.9 11.7 %copy-start.6 = (bf16[512,512]{1,0:T(8,128)(2,1)S(1)}, bf16[512,512]{1,0:T(8,128)(2,1)}, u32[]{:S(2)}) copy-start(bf16[512,512]{1,0:T(8,128)(2,1)} %param.17) | copy-start | bytes 1572868
  14.6 0.9 copy-start.3
  26.0 0.8 copy-start.4
  26.0 0.9 copy-start.2
  27.0 0.9 copy-start.1
  96.2 0.7 copy-start.11
where the time goes:
time: 99.2 us; the launch traced here: 98.7 us
  blocking collectives  82.3 us (83%)
  matrix products  6.91 us (7%)
  local copies, waits for them, and re-layouts  6.16 us (6%)
  between operations  1.7 us (2%)
  other arithmetic  1.61 us (2%)
    all_gather x4, blocking collectives, climb(): gathered = lax.all_gather(piece[None], 'leaf', axis=0, tiled=True)  36.8 us
    all_gather x4, blocking collectives, descend(): gathered = lax.all_gather(outgoing[None], 'leaf', axis=0, tiled=True)  31.9 us
    unnamed x1, blocking collectives  13.6 us
    unnamed x27, local copies, waits for them, and re-layouts  5.69 us
    dot_general x12, matrix products, across(): lax.dot_general(former, latter, (((1,), (1,)), ((), ())), preferred_eleme...  3.42 us
    dot_general x14, matrix products, plain_dot(): return jnp.dot(former, latter, preferred_element_type=jnp.float32)  3.11 us

commit v1 on v0

--- a/solution.py
+++ b/solution.py
@@ -3,6 +3,29 @@
 import jax.numpy as jnp
 from jax import lax
 from jax.sharding import PartitionSpec as P
+
+
+def joined_along(blocks, dim):
+    shape = list(blocks.shape[1:])
+    shape[dim] *= blocks.shape[0]
+    return jnp.moveaxis(blocks, 0, dim).reshape(shape)
+
+
+def grow_blocks(x, axis):
+    size, mine = (lax.axis_size(axis), lax.axis_index(axis))
+    blocks, stride = (x[None], 1)
+    while stride < size:
+        partner_block = lax.ppermute(blocks, axis, [(i, i ^ stride) for i in range(size)])
+        low = mine & stride == 0
+        blocks = jnp.concatenate(
+            [jnp.where(low, blocks, partner_block), jnp.where(low, partner_block, blocks)]
+        )
+        stride *= 2
+    return blocks
+
+
+def collect(x, axis, dim):
+    return joined_along(grow_blocks(x, axis), dim)
 
 
 def across(former, latter):
@@ -77,7 +100,7 @@
     for height in range(1, levels + 1):
         lowest = (height - 1) * block_size
         piece = jnp.stack([summed[:, lowest : lowest + block_size] for summed in contributions])
-        gathered = lax.all_gather(piece[None], "leaf", axis=0, tiled=True)
+        gathered = collect(piece[None], "leaf", 0)
         first = device >> height << height
         total = jnp.sum(lax.dynamic_slice_in_dim(gathered, first, 1 << height, 0), axis=0)
         owner = device % (1 << height) == 0

time: 99.2 us -> 83.4 us (0.84)
  blocking collectives: 82.3 us -> 46 us
  starting transfers between devices: 0 us -> 12.3 us
  waiting for transfers between devices: 0 us -> 8.26 us
    all_gather x4 -> x0, blocking collectives: 36.8 us -> none  [climb(): gathered = lax.all_gather(piece[None], 'leaf', axis=0, tiled=True)]
    ppermute x0 -> x8, starting transfers between devices: none -> 12.3 us  [grow_blocks(): lax.ppermute(blocks, axis, [(i, i ^ stride) for i in range(size)])]
    ppermute x0 -> x8, waiting for transfers between devices: none -> 8.26 us  [grow_blocks(): lax.ppermute(blocks, axis, [(i, i ^ stride) for i in range(size)])]
  transfers between devices with their start and end apart: 0 -> 8, of which waited for: 0 -> 6; matrix products, arithmetic and copies ran while one was open for 0% -> 4% of each run, Pallas kernels for 0% -> 0%
where the time goes in v1:
time: 83.4 us; the launch traced here: 83 us
  blocking collectives  46 us (55%)
  starting transfers between devices  12.3 us (15%)
  waiting for transfers between devices  8.26 us (10%)
  matrix products  6.92 us (8%)
  local copies, waits for them, and re-layouts  6.04 us (7%)
  other arithmetic  1.79 us (2%)
  between operations  1.74 us (2%)
    all_gather x4, blocking collectives, descend(): gathered = lax.all_gather(outgoing[None], 'leaf', axis=0, tiled=True)  32.4 us
    unnamed x1, blocking collectives  13.6 us
    ppermute x8, starting transfers between devices, grow_blocks(): lax.ppermute(blocks, axis, [(i, i ^ stride) for i in range(size)])  12.3 us
    ppermute x8, waiting for transfers between devices, grow_blocks(): lax.ppermute(blocks, axis, [(i, i ^ stride) for i in range(size)])  8.26 us
    unnamed x27, local copies, waits for them, and re-layouts  5.57 us
    dot_general x12, matrix products, across(): lax.dot_general(former, latter, (((1,), (1,)), ((), ())), preferred_eleme...  3.43 us
    dot_general x14, matrix products, plain_dot(): return jnp.dot(former, latter, preferred_element_type=jnp.float32)  3.11 us
  transfers between devices with their start and end apart: 8, of which 6 were waited for; matrix products, arithmetic and copies ran while one was open for 4% of the time, Pallas kernels for 0%

profile of v1, /device:TPU:0, one launch (start us, length us, event | category | flops | bytes accessed | tf_op | source)
XLA Modules:
  0.0 83.0 jit_solution(11813431986653702561)
XLA Ops:
  0.6 0.0 copy-start
  0.7 0.7 broadcast_subtract_fusion
  1.5 0.9 %fusion.196 = (bf16[128,128]{0,1:T(8,128)(2,1)S(1)}, f32[128,128]{0,1:T(8,128)S(1)}) fusion(bf16[512,512]{1,0:T(8,128)(2,1)} %param.16, f32[128,512]{0,1:T(8,128)S(1)} %fusion.15), kind=kOutput, calls=%fused_computation.237 | convolution fusion | flops 4227072 | bytes 229376 | tf_op jit(solution)/shard_map/dot_general | solution.py:32
  2.4 0.2 fusion.197
  2.5 0.2 convolution_subtract_fusion.5
  2.7 0.5 copy-done.9
  3.2 0.2 slice_reduce_fusion
  3.4 0.1 broadcast_bitcast_fusion.1
  3.5 0.2 convolution_multiply_fusion.1
  3.8 3.0 %collective-permute-start = (f32[1,1,1,128,128]{4,3,2,1,0:T(8,128)S(1)}, f32[1,1,1,128,128]{4,3,2,1,0:T(8,128)S(1)}, u32[]{:S(2)}, u32[]{:S(2)}) collective-permute-start(f32[1,1,1,128,128]{4,3,2,1,0:T(8,128)S(1)} %slice_bitcast_fusion.1), channel_id=1, source_target_pairs={{0,8},{8,0},{16,24},{24,16},{1,9},{9,1},{17,25},{25,17},{2,10},{10... | collective-permute-start | bytes 196616 | tf_op jit(solution)/shard_map/ppermute | solution.py:18
  6.8 0.4 convolution_bitcast_fusion
  7.2 0.2 fusion.187
  7.4 0.3 fusion.188
  7.8 0.4 fusion.191
  8.2 0.4 fusion.12
  8.5 0.6 copy-done.1
  9.1 0.2 convolution_multiply_fusion
  9.3 0.8 collective-permute-start.4
  10.1 0.1 broadcast_bitcast_fusion
  10.3 1.6 %collective-permute-start.1 = (f32[2,1,1,128,128]{4,3,2,1,0:T(8,128)S(1)}, f32[2,1,1,128,128]{4,3,2,1,0:T(8,128)S(1)}, u32[]{:S(2)}, u32[]{:S(2)}) collective-permute-start(f32[2,1,1,128,128]{4,3,2,1,0:T(8,128)S(1)} %pad_maximum_fusion.4), channel_id=1, source_target_pairs={{0,16},{8,24},{16,0},{24,8},{1,17},{9,25},{17,1},{25,9},{2,18},{10... | collective-permute-start | bytes 393224 | tf_op jit(solution)/shard_map/ppermute | solution.py:18
  11.9 1.8 %collective-permute-done.4 = f32[1,1,1,128,128]{4,3,2,1,0:T(8,128)S(1)} collective-permute-done((f32[1,1,1,128,128]{4,3,2,1,0:T(8,128)S(1)}, f32[1,1,1,128,128]{4,3,2,1,0:T(8,128)S(1)}, u32[]{:S(2)}, u32[]{:S(2)}) %collective-permute-start.4) | collective-permute-done | bytes 65568 | tf_op jit(solution)/shard_map/ppermute | solution.py:18
  13.7 1.6 %collective-permute-start.5 = (f32[2,1,1,128,128]{4,3,2,1,0:T(8,128)S(1)}, f32[2,1,1,128,128]{4,3,2,1,0:T(8,128)S(1)}, u32[]{:S(2)}, u32[]{:S(2)}) collective-permute-start(f32[2,1,1,128,128]{4,3,2,1,0:T(8,128)S(1)} %pad_maximum_fusion.6), channel_id=1, source_target_pairs={{0,16},{8,24},{16,0},{24,8},{1,17},{9,25},{17,1},{25,9},{2,18},{10... | collective-permute-start | bytes 393224 | tf_op jit(solution)/shard_map/ppermute | solution.py:18
  15.3 0.6 collective-permute-done.1
  15.9 2.9 %collective-permute-done.5 = f32[2,1,1,128,128]{4,3,2,1,0:T(8,128)S(1)} collective-permute-done((f32[2,1,1,128,128]{4,3,2,1,0:T(8,128)S(1)}, f32[2,1,1,128,128]{4,3,2,1,0:T(8,128)S(1)}, u32[]{:S(2)}, u32[]{:S(2)}) %collective-permute-start.5) | collective-permute-done | bytes 131104 | tf_op jit(solution)/shard_map/ppermute | solution.py:18
  18.8 0.1 fusion.23
  18.9 0.8 copy-done.5
  19.6 0.1 fusion.128
  19.7 0.0 copy-done.3
  19.8 0.1 fusion.96
  19.9 0.8 copy-done.2
  20.7 0.2 fusion.103
  20.9 0.8 collective-permute-start.6
  21.6 0.1 broadcast_bitcast_fusion.2
  21.7 0.7 copy-done.11
  22.4 0.6 dynamic-slice.2
  23.6 1.4 %collective-permute-start.2 = (f32[1,1,1,128,128]{4,3,2,1,0:T(8,128)S(1)}, f32[1,1,1,128,128]{4,3,2,1,0:T(8,128)S(1)}, u32[]{:S(2)}, u32[]{:S(2)}) collective-permute-start(f32[1,1,1,128,128]{4,3,2,1,0:T(8,128)S(1)} %get-tuple-element.32), channel_id=1, source_target_pairs={{0,8},{8,0},{16,24},{24,16},{1,9},{9,1},{17,25},{25,17},{2,10},{10... | collective-permute-start | bytes 196616 | tf_op jit(solution)/shard_map/ppermute | solution.py:18
  25.0 0.8 collective-permute-done.6
  25.8 1.6 %collective-permute-start.7 = (f32[2,1,1,128,128]{4,3,2,1,0:T(8,128)S(1)}, f32[2,1,1,128,128]{4,3,2,1,0:T(8,128)S(1)}, u32[]{:S(2)}, u32[]{:S(2)}) collective-permute-start(f32[2,1,1,128,128]{4,3,2,1,0:T(8,128)S(1)} %pad_maximum_fusion.7), channel_id=1, source_target_pairs={{0,16},{8,24},{16,0},{24,8},{1,17},{9,25},{17,1},{25,9},{2,18},{10... | collective-permute-start | bytes 393224 | tf_op jit(solution)/shard_map/ppermute | solution.py:18
  27.4 0.6 collective-permute-done.2
  28.0 1.6 %collective-permute-start.3 = (f32[2,1,1,128,128]{4,3,2,1,0:T(8,128)S(1)}, f32[2,1,1,128,128]{4,3,2,1,0:T(8,128)S(1)}, u32[]{:S(2)}, u32[]{:S(2)}) collective-permute-start(f32[2,1,1,128,128]{4,3,2,1,0:T(8,128)S(1)} %pad_maximum_fusion.5), channel_id=1, source_target_pairs={{0,16},{8,24},{16,0},{24,8},{1,17},{9,25},{17,1},{25,9},{2,18},{10... | collective-permute-start | bytes 393224 | tf_op jit(solution)/shard_map/ppermute | solution.py:18
  29.6 1.7 %collective-permute-done.7 = f32[2,1,1,128,128]{4,3,2,1,0:T(8,128)S(1)} collective-permute-done((f32[2,1,1,128,128]{4,3,2,1,0:T(8,128)S(1)}, f32[2,1,1,128,128]{4,3,2,1,0:T(8,128)S(1)}, u32[]{:S(2)}, u32[]{:S(2)}) %collective-permute-start.7) | collective-permute-done | bytes 131104 | tf_op jit(solution)/shard_map/ppermute | solution.py:18
  31.3 0.1 fusion.129
  31.4 0.1 fusion.4
  31.6 9.0 %all-gather.2 = bf16[512,128]{1,0:T(8,128)(2,1)S(1)} all-gather(bf16[128,128]{1,0:T(8,128)(2,1)S(1)} %fusion.4), channel_id=4, replica_groups=mesh['leaf'=4,'src'=8] {'leaf'}, dimensions={0}, use_global_device_ids=true | all-gather | bytes 163840 | tf_op jit(solution)/shard_map/all_gather | solution.py:120
  40.6 0.1 fusion.5
  40.7 7.3 %all-gather.3 = bf16[512,128]{1,0:T(8,128)(2,1)S(1)} all-gather(bf16[128,128]{1,0:T(8,128)(2,1)S(1)} %fusion.5), channel_id=5, replica_groups=mesh['leaf'=4,'src'=8] {'leaf'}, dimensions={0}, use_global_device_ids=true | all-gather | bytes 163840 | tf_op jit(solution)/shard_map/all_gather | solution.py:120
  48.1 0.3 convolution_subtract_fusion
  48.4 0.2 fusion.198
  48.6 0.3 convolution_convert_fusion.1
  48.9 8.6 %all-gather = bf16[512,128]{1,0:T(8,128)(2,1)S(1)} all-gather(bf16[128,128]{1,0:T(8,128)(2,1)S(1)} %convolution_convert_fusion.1), channel_id=2, replica_groups=mesh['leaf'=4,'src'=8] {'leaf'}, dimensions={0}, use_global_device_ids=true | all-gather | bytes 163840 | tf_op jit(solution)/shard_map/all_gather | solution.py:120
  57.5 0.3 convolution_convert_fusion
  57.8 7.5 %all-gather.1 = bf16[512,128]{1,0:T(8,128)(2,1)S(1)} all-gather(bf16[128,128]{1,0:T(8,128)(2,1)S(1)} %convolution_convert_fusion), channel_id=3, replica_groups=mesh['leaf'=4,'src'=8] {'leaf'}, dimensions={0}, use_global_device_ids=true | all-gather | bytes 163840 | tf_op jit(solution)/shard_map/all_gather | solution.py:120
  65.3 0.2 convolution_subtract_fusion.1
  65.6 0.1 fusion.200
  65.7 0.3 fusion.201
  66.0 0.3 fusion.204
  66.3 0.3 fusion.9
  66.6 0.2 fusion.199
  66.8 0.2 convolution_subtract_fusion.8
  67.1 0.1 multiply_reduce_fusion
  67.2 0.8 %copy.21 = f32[128,512]{1,0:T(8,128)} copy(f32[128,512]{0,1:T(8,128)S(1)} %get-tuple-element.17) | data formatting | bytes 524288
  68.0 0.8 %copy.22 = f32[128,512]{1,0:T(8,128)} copy(f32[128,512]{0,1:T(8,128)S(1)} %get-tuple-element.18) | data formatting | bytes 524288
  68.9 13.6 %all-reduce.2 = f32[512]{0:T(512)S(1)} all-reduce(f32[512]{0:T(512)S(1)} %get-tuple-element.16), channel_id=6, replica_groups=mesh['leaf'=4,'src'=8] {'src'}, use_global_device_ids=true, to_apply=%region_7.8.clone | all-reduce | flops 512 | bytes 4096
  82.5 0.6 dynamic-slice_multiply_fusion
  (48 shorter events, 0.4 us)
Async XLA Ops:
  0.6 2.9 %copy-start = (bf16[256,512]{1,0:T(8,128)(2,1)S(1)}, bf16[256,512]{1,0:T(8,128)(2,1)}, u32[]{:S(2)}) copy-start(bf16[256,512]{1,0:T(8,128)(2,1)} %param.19) | copy-start | bytes 786436
  0.6 1.7 %copy-start.7 = (bf16[512,512]{1,0:T(8,128)(2,1)S(1)}, bf16[512,512]{1,0:T(8,128)(2,1)}, u32[]{:S(2)}) copy-start(bf16[512,512]{1,0:T(8,128)(2,1)} %param.16) | copy-start | bytes 1572868
  2.5 0.7 copy-start.9
  3.5 3.9 %copy-start.6 = (bf16[512,512]{1,0:T(8,128)(2,1)S(1)}, bf16[512,512]{1,0:T(8,128)(2,1)}, u32[]{:S(2)}) copy-start(bf16[512,512]{1,0:T(8,128)(2,1)} %param.17) | copy-start | bytes 1572868
  3.8 3.1 %copy-start.8 = (f32[128,128]{1,0:T(8,128)S(1)}, f32[128,128]{1,0:T(8,128)}, u32[]{:S(2)}) copy-start(f32[128,128]{1,0:T(8,128)} %param.14) | copy-start | bytes 196612
  3.8 3.0 %copy-start.10 = (s32[128]{0:T(128)S(1)}, s32[128]{0:T(128)}, u32[]{:S(2)}) copy-start(s32[128]{0:T(128)} %param.13) | copy-start | bytes 1540
  3.8 3.4 %copy-start.4 = (bf16[4,128,128]{2,1,0:T(8,128)(2,1)S(1)}, bf16[4,128,128]{2,1,0:T(8,128)(2,1)}, u32[]{:S(2)}) copy-start(bf16[4,128,128]{2,1,0:T(8,128)(2,1)} %param.18) | copy-start | bytes 393220
  3.8 6.4 %collective-permute-start = (f32[1,1,1,128,128]{4,3,2,1,0:T(8,128)S(1)}, f32[1,1,1,128,128]{4,3,2,1,0:T(8,128)S(1)}, u32[]{:S(2)}, u32[]{:S(2)}) collective-permute-start(f32[1,1,1,128,128]{4,3,2,1,0:T(8,128)S(1)} %slice_bitcast_fusion.1), channel_id=1, source_target_pairs={{0,8},{8,0},{16,24},{24,16},{1,9},{9,1},{17,25},{25,17},{2,10},{10... | collective-permute-start | bytes 196616 | tf_op jit(solution)/shard_map/ppermute | solution.py:18
  8.1 1.0 %copy-start.1 = (bf16[512,256]{1,0:T(8,128)(2,1)S(1)}, bf16[512,256]{1,0:T(8,128)(2,1)}, u32[]{:S(2)}) copy-start(bf16[512,256]{1,0:T(8,128)(2,1)} %param.20) | copy-start | bytes 786436
  9.3 4.3 %collective-permute-start.4 = (f32[1,1,1,128,128]{4,3,2,1,0:T(8,128)S(1)}, f32[1,1,1,128,128]{4,3,2,1,0:T(8,128)S(1)}, u32[]{:S(2)}, u32[]{:S(2)}) collective-permute-start(f32[1,1,1,128,128]{4,3,2,1,0:T(8,128)S(1)} %slice_bitcast_fusion), channel_id=1, source_target_pairs={{0,8},{8,0},{16,24},{24,16},{1,9},{9,1},{17,25},{25,17},{2,10},{10... | collective-permute-start | bytes 196616 | tf_op jit(solution)/shard_map/ppermute | solution.py:18
  10.3 5.6 %collective-permute-start.1 = (f32[2,1,1,128,128]{4,3,2,1,0:T(8,128)S(1)}, f32[2,1,1,128,128]{4,3,2,1,0:T(8,128)S(1)}, u32[]{:S(2)}, u32[]{:S(2)}) collective-permute-start(f32[2,1,1,128,128]{4,3,2,1,0:T(8,128)S(1)} %pad_maximum_fusion.4), channel_id=1, source_target_pairs={{0,16},{8,24},{16,0},{24,8},{1,17},{9,25},{17,1},{25,9},{2,18},{10... | collective-permute-start | bytes 393224 | tf_op jit(solution)/shard_map/ppermute | solution.py:18
  13.7 5.0 %collective-permute-start.5 = (f32[2,1,1,128,128]{4,3,2,1,0:T(8,128)S(1)}, f32[2,1,1,128,128]{4,3,2,1,0:T(8,128)S(1)}, u32[]{:S(2)}, u32[]{:S(2)}) collective-permute-start(f32[2,1,1,128,128]{4,3,2,1,0:T(8,128)S(1)} %pad_maximum_fusion.6), channel_id=1, source_target_pairs={{0,16},{8,24},{16,0},{24,8},{1,17},{9,25},{17,1},{25,9},{2,18},{10... | collective-permute-start | bytes 393224 | tf_op jit(solution)/shard_map/ppermute | solution.py:18
  18.8 0.8 %copy-start.5 = (bf16[2,128,128]{2,1,0:T(8,128)(2,1)S(1)}, bf16[2,128,128]{2,1,0:T(8,128)(2,1)}, u32[]{:S(2)}) copy-start(bf16[2,128,128]{2,1,0:T(8,128)(2,1)} %param.21) | copy-start | bytes 196612
  18.8 0.9 %copy-start.3 = (bf16[2,128,256]{2,1,0:T(8,128)(2,1)S(1)}, bf16[2,128,256]{2,1,0:T(8,128)(2,1)}, u32[]{:S(2)}) copy-start(bf16[2,128,256]{2,1,0:T(8,128)(2,1)} %param.23) | copy-start | bytes 393220
  19.8 0.9 %copy-start.2 = (bf16[2,256,128]{2,1,0:T(8,128)(2,1)S(1)}, bf16[2,256,128]{2,1,0:T(8,128)(2,1)}, u32[]{:S(2)}) copy-start(bf16[2,256,128]{2,1,0:T(8,128)(2,1)} %param.22) | copy-start | bytes 393220
  20.9 4.9 %collective-permute-start.6 = (f32[1,1,1,128,128]{4,3,2,1,0:T(8,128)S(1)}, f32[1,1,1,128,128]{4,3,2,1,0:T(8,128)S(1)}, u32[]{:S(2)}, u32[]{:S(2)}) collective-permute-start(f32[1,1,1,128,128]{4,3,2,1,0:T(8,128)S(1)} %get-tuple-element.31), channel_id=1, source_target_pairs={{0,8},{8,0},{16,24},{24,16},{1,9},{9,1},{17,25},{25,17},{2,10},{10... | collective-permute-start | bytes 196616 | tf_op jit(solution)/shard_map/ppermute | solution.py:18
  21.7 0.7 copy-start.11
  23.6 4.3 %collective-permute-start.2 = (f32[1,1,1,128,128]{4,3,2,1,0:T(8,128)S(1)}, f32[1,1,1,128,128]{4,3,2,1,0:T(8,128)S(1)}, u32[]{:S(2)}, u32[]{:S(2)}) collective-permute-start(f32[1,1,1,128,128]{4,3,2,1,0:T(8,128)S(1)} %get-tuple-element.32), channel_id=1, source_target_pairs={{0,8},{8,0},{16,24},{24,16},{1,9},{9,1},{17,25},{25,17},{2,10},{10... | collective-permute-start | bytes 196616 | tf_op jit(solution)/shard_map/ppermute | solution.py:18
  25.8 5.5 %collective-permute-start.7 = (f32[2,1,1,128,128]{4,3,2,1,0:T(8,128)S(1)}, f32[2,1,1,128,128]{4,3,2,1,0:T(8,128)S(1)}, u32[]{:S(2)}, u32[]{:S(2)}) collective-permute-start(f32[2,1,1,128,128]{4,3,2,1,0:T(8,128)S(1)} %pad_maximum_fusion.7), channel_id=1, source_target_pairs={{0,16},{8,24},{16,0},{24,8},{1,17},{9,25},{17,1},{25,9},{2,18},{10... | collective-permute-start | bytes 393224 | tf_op jit(solution)/shard_map/ppermute | solution.py:18
  28.0 20.6 %collective-permute-start.3 = (f32[2,1,1,128,128]{4,3,2,1,0:T(8,128)S(1)}, f32[2,1,1,128,128]{4,3,2,1,0:T(8,128)S(1)}, u32[]{:S(2)}, u32[]{:S(2)}) collective-permute-start(f32[2,1,1,128,128]{4,3,2,1,0:T(8,128)S(1)} %pad_maximum_fusion.5), channel_id=1, source_target_pairs={{0,16},{8,24},{16,0},{24,8},{1,17},{9,25},{17,1},{25,9},{2,18},{10... | collective-permute-start | bytes 393224 | tf_op jit(solution)/shard_map/ppermute | solution.py:18
